TPU v7x, 512 devices: a whole 4x4x16 slice. The times are simulated.
512 devices in a mesh: ctx: 32 (over z_hi, y, x), exp: 16 (over z_lo, core).
Axes of the slice: x: 4, y: 4, z: 16 (z_hi: 2, z_lo: 8; z = z_hi * 8 + z_lo), core: 2. Of those that a mesh axis runs over, the one named last changes fastest.
Arguments:
- hidden_in: bfloat16 [4096, 2880], P('ctx'), may hold values from -6 to 6
- query_input: bfloat16 [4096, 2048], P('ctx', 'exp'), may hold values from -16 to 16
- key_heads_input: bfloat16 [4096, 256], P('ctx'), may hold values from -16 to 16
- value_heads_input: bfloat16 [4096, 256], P('ctx'), may hold values from -6 to 6
- sink_logits: float32 [32], P('exp'), may hold values from 0 to 4
- out_proj: bfloat16 [2048, 2880], P('exp'), may hold values from -0.125 to 0.125
- norm_gain: float32 [2880], replicated, may hold values from 0.5 to 1.5
- expert_ids: int32 [4096, 4], P('ctx'), may hold values from 0 to 31, all different within a row; in each aligned block of 128 rows (0 to 127, 128 to 255, ...) at most 20 rows name the same one
- expert_gates: float32 [4096, 4], P('ctx'), may hold values from 0.1 to 1
- gate_up: bfloat16 [32, 2880, 2, 2880], P('ctx', None, None, 'exp'), may hold values from -0.109375 to 0.109375
- down_proj: bfloat16 [32, 2880, 2880], P('ctx', 'exp'), may hold values from -0.109375 to 0.109375
Outputs:
- layer_out: bfloat16 [4096, 2880], P('ctx', 'exp')
Inputs may be any that keep to these rules, and one draw needn't show every extreme that they name: `expert_ids`: each token names 4 different experts; within the 128 tokens of one device no expert is named by more than 20 tokens.
All inputs are finite; a program needn't handle non-finite values.
Results may differ from a plain program's by a relative error of at most 0.02.
Values may be sent and summed in bfloat16 or wider, within the bound.
No kernel may reach another device: no remote copies, remote signals or barrier semaphores. Data moves between devices by JAX's collectives and lax.ppermute only.
A program may use at most 64 MiB of HBM per device.

v0:
```python
import functools
import math
import jax
import jax.numpy as jnp
import numpy as np
from jax import lax
from jax.sharding import Mesh, PartitionSpec as P

D = 2880
QUERY_HEADS = 32
KEY_VALUE_HEADS = 4
HEAD_SIZE = 64
yarn_base = 150000.0
yarn_factor = 32.0
yarn_initial = 4096.0
beta_fast = 32.0
beta_slow = 1.0
neg_large = -1e30


def yarn_frequencies(head_dim):
    half_dim = head_dim // 2

    def correction(rotations):
        return (
            head_dim
            * math.log(yarn_initial / (rotations * 2.0 * math.pi))
            / (2.0 * math.log(yarn_base))
        )

    lower_dim = max(math.floor(correction(beta_fast)), 0)
    upper_dim = min(math.ceil(correction(beta_slow)), head_dim - 1)
    extrap_freq = 1.0 / yarn_base ** (np.arange(0, head_dim, 2) / head_dim)
    interp_freq = extrap_freq / yarn_factor
    ramp_part = np.clip((np.arange(half_dim) - lower_dim) / (upper_dim - lower_dim), 0.0, 1.0)
    extrap_share = 1.0 - ramp_part
    return (interp_freq * (1.0 - extrap_share) + extrap_freq * extrap_share).astype(np.float32)


def rotate_with_yarn(heads_in, token_positions):
    head_dim = heads_in.shape[-1]
    freqs = jnp.asarray(yarn_frequencies(head_dim))
    angles = token_positions.astype(jnp.float32)[:, None] * freqs[None, :]
    factor = 0.1 * math.log(yarn_factor) + 1.0
    cosine = (jnp.cos(angles) * factor)[:, None, :]
    sine = (jnp.sin(angles) * factor)[:, None, :]
    first_half = heads_in[..., : head_dim // 2]
    second_half = heads_in[..., head_dim // 2 :]
    return jnp.concatenate(
        [first_half * cosine - second_half * sine, second_half * cosine + first_half * sine],
        axis=-1,
    )


def route_slots(ids_block, n_experts):
    flat_ids = ids_block.reshape(-1)
    onehot = (flat_ids[:, None] == jnp.arange(n_experts, dtype=jnp.int32)[None, :]).astype(
        jnp.int32
    )
    ranks = jnp.cumsum(onehot, axis=0) - onehot
    return jnp.sum(ranks * onehot, axis=1).reshape(ids_block.shape)


CTX = ("zh", "y", "x")
EXP = ("zl", "c")


def per_device(
    hidden_in,
    query_input,
    key_heads_input,
    value_heads_input,
    sink_logits,
    out_proj,
    norm_gain,
    expert_ids,
    expert_gates,
    gate_up,
    down_proj,
    *,
    ctx_count,
    zl_count,
    c_count
):
    tok_rows = hidden_in.shape[0]
    exp_count = zl_count * c_count
    local_heads = query_input.shape[1] // HEAD_SIZE
    ctx_index = lax.axis_index(CTX)
    exp_index = lax.axis_index(EXP)
    token_positions = ctx_index * tok_rows + jnp.arange(tok_rows, dtype=jnp.int32)
    q_rot = rotate_with_yarn(
        query_input.astype(jnp.float32).reshape(tok_rows, local_heads, HEAD_SIZE), token_positions
    ).astype(jnp.bfloat16)
    shared_key_head = exp_index * local_heads // (QUERY_HEADS // KEY_VALUE_HEADS)
    key_block = lax.dynamic_slice_in_dim(key_heads_input, shared_key_head * HEAD_SIZE, HEAD_SIZE, 1)
    value_block = lax.dynamic_slice_in_dim(
        value_heads_input, shared_key_head * HEAD_SIZE, HEAD_SIZE, 1
    )
    key_rot = (
        rotate_with_yarn(
            key_block.astype(jnp.float32).reshape(tok_rows, 1, HEAD_SIZE), token_positions
        )
        .reshape(tok_rows, HEAD_SIZE)
        .astype(jnp.bfloat16)
    )
    key_value = jnp.concatenate([key_rot, value_block], axis=1)
    score_scale = 1.0 / math.sqrt(HEAD_SIZE)
    block_part = lax.all_gather(key_value, CTX, axis=0, tiled=True)
    run_max = jnp.broadcast_to(sink_logits[:, None], (local_heads, tok_rows))
    run_total = jnp.ones((local_heads, tok_rows), jnp.float32)
    key_count = block_part.shape[0]
    key_part = block_part[:, :HEAD_SIZE]
    value_part = block_part[:, HEAD_SIZE:].astype(jnp.float32)
    scores = (
        jnp.einsum("rhd,kd->hrk", q_rot, key_part, preferred_element_type=jnp.float32) * score_scale
    )
    key_pos = jnp.arange(key_count, dtype=jnp.int32)
    visible = token_positions[:, None] >= key_pos[None, :]
    scores = jnp.where(visible[None, :, :], scores, neg_large)
    new_max = jnp.maximum(run_max, jnp.max(scores, axis=2))
    weights = jnp.exp(scores - new_max[:, :, None])
    factor = jnp.exp(run_max - new_max)
    run_total = run_total * factor + jnp.sum(weights, axis=2)
    run_sum = jnp.einsum("hrk,kd->hrd", weights, value_part, precision=lax.Precision.HIGHEST)
    attended = (
        (run_sum / run_total[:, :, None])
        .transpose(1, 0, 2)
        .reshape(tok_rows, local_heads * HEAD_SIZE)
        .astype(jnp.bfloat16)
    )
    col_width = D // exp_count
    head_part = jnp.dot(attended, out_proj, preferred_element_type=jnp.float32).astype(jnp.bfloat16)
    head_part = head_part.reshape(tok_rows, zl_count, c_count, col_width).transpose(2, 1, 0, 3)
    head_part = lax.psum_scatter(head_part, "c", scatter_dimension=0, tiled=True)[0]
    head_cols = lax.psum_scatter(head_part, "zl", scatter_dimension=0, tiled=True)[0]
    residual_cols = lax.dynamic_slice_in_dim(hidden_in, exp_index * col_width, col_width, 1).astype(
        jnp.float32
    ) + head_cols.astype(jnp.float32)
    square_sum = lax.psum(jnp.sum(residual_cols * residual_cols, axis=1), EXP)
    gain_cols = lax.dynamic_slice_in_dim(norm_gain, exp_index * col_width, col_width, 0)
    normed_cols = (
        residual_cols * lax.rsqrt(square_sum / D + 1e-05)[:, None] * gain_cols[None, :]
    ).astype(jnp.bfloat16)
    exp_local = gate_up.shape[0]
    n_experts = exp_local * ctx_count
    top_count = expert_ids.shape[1]
    capacity = max(2, tok_rows * top_count * 5 // (4 * n_experts))
    slot_index = route_slots(expert_ids, n_experts)
    dest_row = expert_ids * capacity + slot_index
    spread_rows = jnp.broadcast_to(
        normed_cols[:, None, :], (tok_rows, top_count, col_width)
    ).reshape(tok_rows * top_count, col_width)
    send_rows = (
        jnp.zeros((n_experts * capacity, col_width), jnp.bfloat16)
        .at[dest_row.reshape(-1)]
        .set(spread_rows)
    )
    bucket_rows = ctx_count * capacity
    unit_count = gate_up.shape[-1]
    received = lax.all_to_all(
        send_rows.reshape(ctx_count, exp_local * capacity, col_width),
        CTX,
        split_axis=0,
        concat_axis=0,
        tiled=True,
    ).reshape(bucket_rows, col_width)
    gathered = lax.all_gather(received, "zl", axis=0, tiled=False)
    gathered = lax.all_gather(gathered, "c", axis=0, tiled=False)
    weights_flat = gate_up.reshape(zl_count, c_count, col_width, 2 * unit_count)
    gate_up_out = jnp.einsum(
        "czrk,zckf->rf", gathered, weights_flat, preferred_element_type=jnp.float32
    )
    gate_up_out = gate_up_out.reshape(bucket_rows, 2, unit_count)
    gate_value = gate_up_out[:, 0]
    up_value = gate_up_out[:, 1]
    activated = ((up_value + 1.0) * gate_value * jax.nn.sigmoid(1.702 * gate_value)).astype(
        jnp.bfloat16
    )
    down_local = down_proj.reshape(unit_count, zl_count, c_count, col_width)
    partial_value = jnp.einsum(
        "rf,fzcd->czrd", activated, down_local, preferred_element_type=jnp.float32
    ).astype(jnp.bfloat16)
    partial_value = lax.psum_scatter(partial_value, "c", scatter_dimension=0, tiled=True)[0]
    expert_cols = lax.psum_scatter(partial_value, "zl", scatter_dimension=0, tiled=True)[0]
    returned = lax.all_to_all(
        expert_cols.reshape(ctx_count, capacity, col_width),
        CTX,
        split_axis=0,
        concat_axis=0,
        tiled=True,
    )
    picked_rows = returned.reshape(n_experts * capacity, col_width)[dest_row]
    moe_cols = jnp.sum(expert_gates[:, :, None] * picked_rows.astype(jnp.float32), axis=1)
    return (residual_cols + moe_cols).astype(jnp.bfloat16)


def solution(mesh):
    ctx_count, exp_count = mesh.devices.shape
    zh, y, x = (mesh.devices.shape[0] // 16, 4, 4)
    c_count = 2
    zl_count = exp_count // c_count
    fine = Mesh(mesh.devices.reshape(zh, y, x, zl_count, c_count), ("zh", "y", "x", "zl", "c"))
    placed = (
        P(CTX, None),
        P(CTX, EXP),
        P(CTX, None),
        P(CTX, None),
        P(EXP),
        P(EXP, None),
        P(),
        P(CTX, None),
        P(CTX, None),
        P(CTX, None, None, EXP),
        P(CTX, EXP, None),
    )
    return jax.shard_map(
        functools.partial(per_device, ctx_count=ctx_count, zl_count=zl_count, c_count=c_count),
        mesh=fine,
        in_specs=placed,
        out_specs=P(CTX, EXP),
        check_vma=False,
    )
```

profile of v0, /device:TPU:32, one launch (start us, length us, event | category | flops | bytes accessed | tf_op | source)
XLA Modules:
  0.0 534.8 jit_solution(13582523231836904942)
XLA Ops:
  6.5 0.9 constant_dynamic-slice_fusion
  7.7 0.8 fusion.33
  8.5 0.6 pad_maximum_fusion
  9.2 0.8 copy.67
  10.1 0.8 fusion.39
  10.9 0.3 iota_compare_fusion
  11.3 113.0 %all-gather.5.cloned.1.call-done = bf16[4096,128]{0,1:T(8,128)(2,1)} async-done(((bf16[128,128]{0,1:T(8,128)(2,1)}), bf16[4096,128]{0,1:T(8,128)(2,1)}) %all-gather.5.cloned.1.call-update) | async-done | bytes 1048592 | tf_op jit(solution)/shard_map/all_gather | solution.py:108
  124.3 2.0 fusion.45
  126.4 0.6 fusion.2
  127.0 2.1 fusion.13
  129.1 0.3 convolution_convert_fusion
  129.6 1.1 copy.69
  131.1 16.4 %reduce-scatter.11.cloned.1.call-done = bf16[1,8,128,180]{2,1,3,0:T(8,128)(2,1)} async-done(((bf16[2,8,128,180]{2,1,3,0:T(8,128)(2,1)}), bf16[1,8,128,180]{2,1,3,0:T(8,128)(2,1)}) %reduce-scatter.11.cloned.1.call-update) | async-done | bytes 368656 | tf_op jit(solution)/shard_map/reduce_scatter | solution.py:134
  147.5 1.8 copy.70
  149.3 0.8 constant_dynamic-slice_fusion.2
  150.2 0.8 dynamic_slice.15
  151.0 1.1 reduce-window.6
  152.2 0.2 slice_reduce_fusion
  153.0 55.7 %reduce-scatter.15.cloned.1.call-done = bf16[1,128,180]{1,2,0:T(8,128)(2,1)} async-done(((bf16[8,128,180]{1,2,0:T(8,128)(2,1)}), bf16[1,128,180]{1,2,0:T(8,128)(2,1)}) %reduce-scatter.15.cloned.1.call-update) | async-done | bytes 46096
  208.7 0.9 copy.71
  209.7 44.4 %psum.7 = f32[128]{0:T(128)S(1)} all-reduce(f32[128]{0:T(128)S(1)} %multiply_reduce_fusion.1), channel_id=1, replica_groups=mesh['zh'=2,'y'=4,'x'=4,'zl'=8,'c'=2] {'zl','c'}, use_global_device_ids=true, to_apply=%region_8.9 | all-reduce | flops 128 | bytes 1024 | tf_op jit(solution)/shard_map/psum | solution.py:139
  254.2 0.2 reshape.333
  254.4 2.4 scatter_custom_fusion
  256.9 30.0 %all_to_all.10 = bf16[32,20,180]{2,1,0:T(8,128)(2,1)S(1)} all-to-all(bf16[32,20,180]{2,1,0:T(8,128)(2,1)S(1)} %reshape.312), channel_id=1, replica_groups=mesh['zh'=2,'y'=4,'x'=4,'zl'=8,'c'=2] {'zh','y','x'}, dimensions={0} | all-to-all | bytes 460800 | tf_op jit(solution)/shard_map/all_to_all | solution.py:160
  287.1 0.8 copy.78
  288.0 62.0 %all-gather.7.cloned.1.call-done = bf16[8,640,180]{1,2,0:T(8,128)(2,1)} async-done(((bf16[1,640,180]{1,2,0:T(8,128)(2,1)}), bf16[8,640,180]{1,2,0:T(8,128)(2,1)}) %all-gather.7.cloned.1.call-update) | async-done | bytes 1843216 | tf_op jit(solution)/shard_map/all_gather | solution.py:167
  349.9 3.0 copy.79
  353.0 0.2 reduce-scatter.13.cloned.1.call-start
  353.2 1.8 copy.81
  355.0 9.8 %reshape.313 = bf16[8,2,180,360]{2,1,0,3:T(2,128)(2,1)} reshape(bf16[1,2880,2,180]{1,3,2,0:T(8,128)(2,1)S(1)} %copy.81) | data formatting | bytes 4147200 | tf_op jit(solution)/shard_map/reshape | solution.py:169
  364.8 6.4 %reshape.314 = bf16[180,8,2,180]{3,2,1,0:T(2,128)(2,1)S(1)} reshape(bf16[1,180,2880]{2,1,0:T(8,128)(2,1)} %param.23) | data formatting | bytes 2073600 | tf_op jit(solution)/shard_map/reshape | solution.py:179
  371.2 5.6 %all-gather.9.cloned.1.call-done = bf16[16,640,180]{1,0,2:T(8,128)(2,1)} async-done(((bf16[8,640,180]{1,0,2:T(8,128)(2,1)}), bf16[16,640,180]{1,0,2:T(8,128)(2,1)}) %all-gather.9.cloned.1.call-update) | async-done | bytes 3686416 | tf_op jit(solution)/shard_map/all_gather | solution.py:168
  376.8 3.0 copy.80
  379.8 3.0 fusion.8
  382.9 1.8 convert_bitcast_fusion
  384.7 2.6 copy.85
  387.3 0.3 reduce-scatter.17.cloned.1.call-start
  387.5 23.2 %reduce-scatter.13.cloned.1.call-done = bf16[1,8,640,180]{2,1,3,0:T(8,128)(2,1)} async-done(((bf16[2,8,640,180]{2,1,3,0:T(8,128)(2,1)}), bf16[1,8,640,180]{2,1,3,0:T(8,128)(2,1)}) %reduce-scatter.13.cloned.1.call-update) | async-done | bytes 1843216 | tf_op jit(solution)/shard_map/reduce_scatter | solution.py:183
  410.8 3.0 copy.86
  413.8 69.3 %reduce-scatter.17.cloned.1.call-done = bf16[1,640,180]{1,2,0:T(8,128)(2,1)} async-done(((bf16[8,640,180]{1,2,0:T(8,128)(2,1)}), bf16[1,640,180]{1,2,0:T(8,128)(2,1)}) %reduce-scatter.17.cloned.1.call-update) | async-done | bytes 230416
  483.1 1.1 copy.87
  484.2 0.8 reshape_squeeze.3
  485.0 17.0 %all-to-all-start.1 = ((bf16[32,20,180]{2,1,0:T(8,128)(2,1)}), bf16[32,20,180]{2,1,0:T(8,128)(2,1)S(1)}, u32[]{:S(2)}, u32[]{:S(2)}) async-start(bf16[32,20,180]{2,1,0:T(8,128)(2,1)} %reshape_squeeze.3), calls=%async_computation.3 | async-start | bytes 786432 | tf_op jit(solution)/shard_map/all_to_all | solution.py:185
  502.3 22.2 %all-to-all-done.1 = bf16[32,20,180]{2,1,0:T(8,128)(2,1)S(1)} async-done(((bf16[32,20,180]{2,1,0:T(8,128)(2,1)}), bf16[32,20,180]{2,1,0:T(8,128)(2,1)S(1)}, u32[]{:S(2)}, u32[]{:S(2)}) %all-to-all-start.1) | async-done | bytes 230432 | tf_op jit(solution)/shard_map/all_to_all | solution.py:185
  524.6 2.0 gather_fusion
  526.6 0.2 reshape.340
  526.8 0.4 multiply_reduce_fusion
  527.2 0.7 copy.89
  (60 shorter events, 2.8 us)
Async XLA Ops:
  6.5 122.5 %copy-start = (bf16[128,2880]{0,1:T(8,128)(2,1)S(1)}, bf16[128,2880]{0,1:T(8,128)(2,1)}, u32[]{:S(2)}) copy-start(bf16[128,2880]{0,1:T(8,128)(2,1)} %param.18) | copy-start | bytes 2211844
  6.5 119.7 %copy-start.5 = (f32[2]{0:T(128)S(1)}, f32[2]{0:T(128)}, u32[]{:S(2)}) copy-start(f32[2]{0:T(128)} %param.17) | copy-start | bytes 28
  6.5 117.7 %all-gather.5.cloned.1.call-start = ((), (), s32[]{:S(2)}) async-start(), calls=%async_computation.6 | async-start | bytes 1081344 | tf_op jit(solution)/shard_map/all_gather | solution.py:108
  9.2 138.3 %reduce-scatter.11.cloned.1.call-start = ((), (), s32[]{:S(2)}) async-start(), calls=%async_computation.7 | async-start | bytes 1105920 | tf_op jit(solution)/shard_map/reduce_scatter | solution.py:134
  124.3 2.7 copy-start.2
  129.1 1.6 copy-start.3
  130.7 78.0 %reduce-scatter.15.cloned.1.call-start = ((), (), s32[]{:S(2)}) async-start(), calls=%async_computation.11 | async-start | bytes 423936
  149.3 200.7 %all-gather.7.cloned.1.call-start = ((), (), s32[]{:S(2)}) async-start(), calls=%async_computation.8 | async-start | bytes 2119680 | tf_op jit(solution)/shard_map/all_gather | solution.py:167
  287.9 88.9 %all-gather.9.cloned.1.call-start = ((), (), s32[]{:S(2)}) async-start(), calls=%async_computation.10 | async-start | bytes 5529600 | tf_op jit(solution)/shard_map/all_gather | solution.py:168
  353.0 57.8 %reduce-scatter.13.cloned.1.call-start = ((), (), s32[]{:S(2)}) async-start(), calls=%async_computation.9 | async-start | bytes 5529600 | tf_op jit(solution)/shard_map/reduce_scatter | solution.py:183
  376.8 3.0 copy-start.1
  387.3 95.8 %reduce-scatter.17.cloned.1.call-start = ((), (), s32[]{:S(2)}) async-start(), calls=%async_computation.12 | async-start | bytes 2119680
  410.8 91.4 %copy-start.4 = (f32[128,4]{0,1:T(4,128)S(1)}, f32[128,4]{0,1:T(4,128)}, u32[]{:S(2)}) copy-start(f32[128,4]{0,1:T(4,128)} %param.21) | copy-start | bytes 6148
  485.0 39.5 %all-to-all-start.1 = ((bf16[32,20,180]{2,1,0:T(8,128)(2,1)}), bf16[32,20,180]{2,1,0:T(8,128)(2,1)S(1)}, u32[]{:S(2)}, u32[]{:S(2)}) async-start(bf16[32,20,180]{2,1,0:T(8,128)(2,1)} %reshape_squeeze.3), calls=%async_computation.3 | async-start | bytes 786432 | tf_op jit(solution)/shard_map/all_to_all | solution.py:185
Sparse Core Ops, SparseCore 0:
  11.4 112.7 all-gather.4
  130.8 16.6 reduce-scatter.10
  150.3 58.3 reduce-scatter.14
  288.1 61.8 all-gather.6
  353.1 23.7 all-gather.8
  387.4 23.3 reduce-scatter.12
  413.9 69.0 reduce-scatter.16
where the time goes:
time: 535 us
  waiting for transfers between devices  367 us (69%)
  blocking collectives  74.4 us (14%)
  local copies, waits for them, and re-layouts  46.9 us (9%)
  starting transfers between devices  17.6 us (3%)
  between operations  13.8 us (3%)
  matrix products  9.28 us (2%)
    unnamed x9, waiting for transfers between devices  125 us
    all_gather x1, waiting for transfers between devices, per_device(): block_part = lax.all_gather(key_value, CTX, axis=0, tiled=True)  113 us
    all_gather x1, waiting for transfers between devices, per_device(): gathered = lax.all_gather(received, 'zl', axis=0, tiled=False)  62 us
    psum x1, blocking collectives, per_device(): square_sum = lax.psum(jnp.sum(residual_cols * residual_cols, axis=1), EXP)  44.4 us
    all_to_all x1, blocking collectives, per_device(): lax.all_to_all(send_rows.reshape(ctx_count, exp_local * capacity, col_wid...  30 us
    reduce_scatter x1, waiting for transfers between devices, per_device(): lax.psum_scatter(partial_value, 'c', scatter_dimension=0, tiled=True)[0]  23.2 us
    all_to_all x1, waiting for transfers between devices, per_device(): lax.all_to_all(expert_cols.reshape(ctx_count, capacity, col_width), CTX,...  22.2 us
    all_to_all x1, starting transfers between devices, per_device(): lax.all_to_all(expert_cols.reshape(ctx_count, capacity, col_width), CTX,...  17 us
  transfers between devices with their start and end apart: 8, of which 8 were waited for; matrix products, arithmetic and copies ran while one was open for 5% of the time, Pallas kernels for 0%

commit v1 on v0

--- a/solution.py
+++ b/solution.py
@@ -105,7 +105,9 @@
     )
     key_value = jnp.concatenate([key_rot, value_block], axis=1)
     score_scale = 1.0 / math.sqrt(HEAD_SIZE)
-    block_part = lax.all_gather(key_value, CTX, axis=0, tiled=True)
+    block_part = jnp.concatenate(
+        lax.all_to_all(jnp.stack([key_value] * lax.axis_size(CTX)), CTX, 0, 0), axis=0
+    )
     run_max = jnp.broadcast_to(sink_logits[:, None], (local_heads, tok_rows))
     run_total = jnp.ones((local_heads, tok_rows), jnp.float32)
     key_count = block_part.shape[0]

time: 535 us -> 492 us (0.920)
  waiting for transfers between devices: 367 us -> 305 us
  starting transfers between devices: 17.6 us -> 37.2 us
    all_gather x1 -> x0, waiting for transfers between devices: 113 us -> none  [per_device(): block_part = lax.all_gather(key_value, CTX, axis=0, tiled=True)]
    all_to_all x0 -> x1, waiting for transfers between devices: none -> 57.2 us  [per_device(): lax.all_to_all(jnp.stack([key_value] * lax.axis_size(CTX)), CTX, 0, 0)]
    all_to_all x0 -> x1, starting transfers between devices: none -> 19.7 us  [per_device(): lax.all_to_all(jnp.stack([key_value] * lax.axis_size(CTX)), CTX, 0, 0)]
    reduce_scatter x1, waiting for transfers between devices: 16.4 us -> 10.2 us  [per_device(): lax.psum_scatter(head_part, 'c', scatter_dimension=0, tiled=True)[0]]
    unnamed x9 -> x8, waiting for transfers between devices: 125 us -> 126 us
where the time goes in v1:
time: 492 us; the launch traced here: 491 us
  waiting for transfers between devices  305 us (62%)
  blocking collectives  74.1 us (15%)
  local copies, waits for them, and re-layouts  48.3 us (10%)
  starting transfers between devices  37.2 us (8%)
  between operations  13.9 us (3%)
  matrix products  8.15 us (2%)
    unnamed x8, waiting for transfers between devices  126 us
    all_gather x1, waiting for transfers between devices, per_device(): gathered = lax.all_gather(received, 'zl', axis=0, tiled=False)  61.3 us
    all_to_all x1, waiting for transfers between devices, per_device(): lax.all_to_all(jnp.stack([key_value] * lax.axis_size(CTX)), CTX, 0, 0)  57.2 us
    psum x1, blocking collectives, per_device(): square_sum = lax.psum(jnp.sum(residual_cols * residual_cols, axis=1), EXP)  44 us
    all_to_all x1, blocking collectives, per_device(): lax.all_to_all(send_rows.reshape(ctx_count, exp_local * capacity, col_wid...  30.1 us
    reduce_scatter x1, waiting for transfers between devices, per_device(): lax.psum_scatter(partial_value, 'c', scatter_dimension=0, tiled=True)[0]  23.2 us
    all_to_all x1, waiting for transfers between devices, per_device(): lax.all_to_all(expert_cols.reshape(ctx_count, capacity, col_width), CTX,...  22.2 us
    all_to_all x1, starting transfers between devices, per_device(): lax.all_to_all(jnp.stack([key_value] * lax.axis_size(CTX)), CTX, 0, 0)  19.7 us
  transfers between devices with their start and end apart: 8, of which 8 were waited for; matrix products, arithmetic and copies ran while one was open for 5% of the time, Pallas kernels for 0%

profile of v1, /device:TPU:32, one launch (start us, length us, event | category | flops | bytes accessed | tf_op | source)
XLA Modules:
  0.0 490.9 jit_solution(6888082760616898453)
XLA Ops:
  6.5 0.9 constant_dynamic-slice_fusion
  7.7 0.8 fusion.33
  8.5 1.2 stack.2
  9.8 19.7 %all-to-all-start = ((bf16[32,128,128]{1,2,0:T(8,128)(2,1)}), bf16[32,128,128]{1,2,0:T(8,128)(2,1)S(1)}, u32[]{:S(2)}, u32[]{:S(2)}) async-start(bf16[32,128,128]{1,2,0:T(8,128)(2,1)} %stack.2), calls=%async_computation | async-start | bytes 2097152 | tf_op jit(solution)/shard_map/all_to_all | solution.py:109
  29.5 0.8 copy.66
  30.6 0.3 iota_compare_fusion
  30.9 57.2 %all-to-all-done = bf16[32,128,128]{1,2,0:T(8,128)(2,1)S(1)} async-done(((bf16[32,128,128]{1,2,0:T(8,128)(2,1)}), bf16[32,128,128]{1,2,0:T(8,128)(2,1)S(1)}, u32[]{:S(2)}, u32[]{:S(2)}) %all-to-all-start) | async-done | bytes 1048608 | tf_op jit(solution)/shard_map/all_to_all | solution.py:109
  88.3 0.9 fusion.45
  89.3 0.6 fusion.2
  89.9 2.1 fusion.13
  92.0 0.3 convolution_convert_fusion
  92.5 1.1 copy.68
  94.0 10.2 %reduce-scatter.11.cloned.1.call-done = bf16[1,8,128,180]{2,1,3,0:T(8,128)(2,1)} async-done(((bf16[2,8,128,180]{2,1,3,0:T(8,128)(2,1)}), bf16[1,8,128,180]{2,1,3,0:T(8,128)(2,1)}) %reduce-scatter.11.cloned.1.call-update) | async-done | bytes 368656 | tf_op jit(solution)/shard_map/reduce_scatter | solution.py:136
  104.1 1.8 copy.69
  106.0 0.8 constant_dynamic-slice_fusion.2
  106.9 0.8 dynamic_slice.15
  107.7 1.1 reduce-window.6
  108.8 0.2 slice_reduce_fusion
  109.7 56.1 %reduce-scatter.15.cloned.1.call-done = bf16[1,128,180]{1,2,0:T(8,128)(2,1)} async-done(((bf16[8,128,180]{1,2,0:T(8,128)(2,1)}), bf16[1,128,180]{1,2,0:T(8,128)(2,1)}) %reduce-scatter.15.cloned.1.call-update) | async-done | bytes 46096
  165.7 0.9 copy.70
  166.7 44.0 %psum.7 = f32[128]{0:T(128)S(1)} all-reduce(f32[128]{0:T(128)S(1)} %multiply_reduce_fusion.1), channel_id=1, replica_groups=mesh['zh'=2,'y'=4,'x'=4,'zl'=8,'c'=2] {'zl','c'}, use_global_device_ids=true, to_apply=%region_8.9 | all-reduce | flops 128 | bytes 1024 | tf_op jit(solution)/shard_map/psum | solution.py:141
  210.9 0.2 reshape.339
  211.0 2.4 scatter_custom_fusion
  213.5 30.1 %all_to_all.15 = bf16[32,20,180]{2,1,0:T(8,128)(2,1)S(1)} all-to-all(bf16[32,20,180]{2,1,0:T(8,128)(2,1)S(1)} %reshape.318), channel_id=1, replica_groups=mesh['zh'=2,'y'=4,'x'=4,'zl'=8,'c'=2] {'zh','y','x'}, dimensions={0} | all-to-all | bytes 460800 | tf_op jit(solution)/shard_map/all_to_all | solution.py:162
  243.8 0.8 copy.77
  244.7 61.3 %all-gather.4.cloned.1.call-done = bf16[8,640,180]{1,2,0:T(8,128)(2,1)} async-done(((bf16[1,640,180]{1,2,0:T(8,128)(2,1)}), bf16[8,640,180]{1,2,0:T(8,128)(2,1)}) %all-gather.4.cloned.1.call-update) | async-done | bytes 1843216 | tf_op jit(solution)/shard_map/all_gather | solution.py:169
  306.0 3.0 copy.78
  309.1 0.2 reduce-scatter.13.cloned.1.call-start
  309.3 1.8 copy.80
  311.1 9.8 %reshape.319 = bf16[8,2,180,360]{2,1,0,3:T(2,128)(2,1)} reshape(bf16[1,2880,2,180]{1,3,2,0:T(8,128)(2,1)S(1)} %copy.80) | data formatting | bytes 4147200 | tf_op jit(solution)/shard_map/reshape | solution.py:171
  320.9 6.4 %reshape.320 = bf16[180,8,2,180]{3,2,1,0:T(2,128)(2,1)S(1)} reshape(bf16[1,180,2880]{2,1,0:T(8,128)(2,1)} %param.23) | data formatting | bytes 2073600 | tf_op jit(solution)/shard_map/reshape | solution.py:181
  327.3 5.6 %all-gather.6.cloned.1.call-done = bf16[16,640,180]{1,0,2:T(8,128)(2,1)} async-done(((bf16[8,640,180]{1,0,2:T(8,128)(2,1)}), bf16[16,640,180]{1,0,2:T(8,128)(2,1)}) %all-gather.6.cloned.1.call-update) | async-done | bytes 3686416 | tf_op jit(solution)/shard_map/all_gather | solution.py:170
  332.9 3.0 copy.79
  335.9 3.0 fusion.8
  338.9 1.8 convert_bitcast_fusion
  340.8 2.6 copy.84
  343.3 0.3 reduce-scatter.17.cloned.1.call-start
  343.6 23.2 %reduce-scatter.13.cloned.1.call-done = bf16[1,8,640,180]{2,1,3,0:T(8,128)(2,1)} async-done(((bf16[2,8,640,180]{2,1,3,0:T(8,128)(2,1)}), bf16[1,8,640,180]{2,1,3,0:T(8,128)(2,1)}) %reduce-scatter.13.cloned.1.call-update) | async-done | bytes 1843216 | tf_op jit(solution)/shard_map/reduce_scatter | solution.py:185
  366.9 3.0 copy.85
  369.9 69.4 %reduce-scatter.17.cloned.1.call-done = bf16[1,640,180]{1,2,0:T(8,128)(2,1)} async-done(((bf16[8,640,180]{1,2,0:T(8,128)(2,1)}), bf16[1,640,180]{1,2,0:T(8,128)(2,1)}) %reduce-scatter.17.cloned.1.call-update) | async-done | bytes 230416
  439.3 1.1 copy.86
  440.4 0.8 reshape_squeeze.3
  441.2 16.9 %all-to-all-start.2 = ((bf16[32,20,180]{2,1,0:T(8,128)(2,1)}), bf16[32,20,180]{2,1,0:T(8,128)(2,1)S(1)}, u32[]{:S(2)}, u32[]{:S(2)}) async-start(bf16[32,20,180]{2,1,0:T(8,128)(2,1)} %reshape_squeeze.3), calls=%async_computation.4 | async-start | bytes 786432 | tf_op jit(solution)/shard_map/all_to_all | solution.py:187
  458.5 22.2 %all-to-all-done.2 = bf16[32,20,180]{2,1,0:T(8,128)(2,1)S(1)} async-done(((bf16[32,20,180]{2,1,0:T(8,128)(2,1)}), bf16[32,20,180]{2,1,0:T(8,128)(2,1)S(1)}, u32[]{:S(2)}, u32[]{:S(2)}) %all-to-all-start.2) | async-done | bytes 230432 | tf_op jit(solution)/shard_map/all_to_all | solution.py:187
  480.8 2.0 gather_fusion
  482.8 0.2 reshape.346
  482.9 0.4 multiply_reduce_fusion
  483.3 0.7 copy.88
  (61 shorter events, 3.1 us)
Async XLA Ops:
  6.5 85.5 %copy-start = (bf16[128,2880]{0,1:T(8,128)(2,1)S(1)}, bf16[128,2880]{0,1:T(8,128)(2,1)}, u32[]{:S(2)}) copy-start(bf16[128,2880]{0,1:T(8,128)(2,1)} %param.18) | copy-start | bytes 2211844
  6.5 23.8 %copy-start.3 = (f32[32]{0:T(128)S(1)}, f32[32]{0:T(128)}, u32[]{:S(2)}) copy-start(f32[32]{0:T(128)} %constant.89.clone) | copy-start | bytes 388
  9.8 78.4 %all-to-all-start = ((bf16[32,128,128]{1,2,0:T(8,128)(2,1)}), bf16[32,128,128]{1,2,0:T(8,128)(2,1)S(1)}, u32[]{:S(2)}, u32[]{:S(2)}) async-start(bf16[32,128,128]{1,2,0:T(8,128)(2,1)} %stack.2), calls=%async_computation | async-start | bytes 2097152 | tf_op jit(solution)/shard_map/all_to_all | solution.py:109
  29.5 74.7 %reduce-scatter.11.cloned.1.call-start = ((), (), s32[]{:S(2)}) async-start(), calls=%async_computation.7 | async-start | bytes 1105920 | tf_op jit(solution)/shard_map/reduce_scatter | solution.py:136
  30.9 58.3 %copy-start.5 = (f32[2]{0:T(128)S(1)}, f32[2]{0:T(128)}, u32[]{:S(2)}) copy-start(f32[2]{0:T(128)} %param.17) | copy-start | bytes 28
  92.0 1.6 copy-start.2
  93.6 72.2 %reduce-scatter.15.cloned.1.call-start = ((), (), s32[]{:S(2)}) async-start(), calls=%async_computation.11 | async-start | bytes 423936
  105.9 200.1 %all-gather.4.cloned.1.call-start = ((), (), s32[]{:S(2)}) async-start(), calls=%async_computation.8 | async-start | bytes 2119680 | tf_op jit(solution)/shard_map/all_gather | solution.py:169
  244.6 88.3 %all-gather.6.cloned.1.call-start = ((), (), s32[]{:S(2)}) async-start(), calls=%async_computation.10 | async-start | bytes 5529600 | tf_op jit(solution)/shard_map/all_gather | solution.py:170
  309.1 57.8 %reduce-scatter.13.cloned.1.call-start = ((), (), s32[]{:S(2)}) async-start(), calls=%async_computation.9 | async-start | bytes 5529600 | tf_op jit(solution)/shard_map/reduce_scatter | solution.py:185
  332.9 3.0 copy-start.1
  343.3 95.9 %reduce-scatter.17.cloned.1.call-start = ((), (), s32[]{:S(2)}) async-start(), calls=%async_computation.12 | async-start | bytes 2119680
  366.9 91.5 %copy-start.4 = (f32[128,4]{0,1:T(4,128)S(1)}, f32[128,4]{0,1:T(4,128)}, u32[]{:S(2)}) copy-start(f32[128,4]{0,1:T(4,128)} %param.21) | copy-start | bytes 6148
  441.2 39.4 %all-to-all-start.2 = ((bf16[32,20,180]{2,1,0:T(8,128)(2,1)}), bf16[32,20,180]{2,1,0:T(8,128)(2,1)S(1)}, u32[]{:S(2)}, u32[]{:S(2)}) async-start(bf16[32,20,180]{2,1,0:T(8,128)(2,1)} %reshape_squeeze.3), calls=%async_computation.4 | async-start | bytes 786432 | tf_op jit(solution)/shard_map/all_to_all | solution.py:187
Sparse Core Ops, SparseCore 0:
  93.7 10.3 reduce-scatter.10
  106.9 58.7 reduce-scatter.14
  244.8 61.2 all-gather.3
  309.2 23.6 all-gather.5
  343.5 23.3 reduce-scatter.12
  370.0 69.2 reduce-scatter.16
